TPU v7x, 32 devices: a whole 2x2x4 slice. The times are simulated.
32 devices in a mesh: beam: 2 (over y), band: 16 (over z, x, core).
Axes of the slice: x: 2, y: 2, z: 4, core: 2. Of those that a mesh axis runs over, the one named last changes fastest.
Arguments:
- filterbank: float32 [1024, 6144], P(('beam', 'band')), parts along dimension 0, may hold values from -40 to 40
- offsets: int32 [9, 512], P(None, 'band'), may hold values from 0 to 255, as said below
- widths: int32 [8], replicated, may hold values from 1 to 128, as said below
Outputs:
- detection: float32 [1024, 2048], P(('beam', 'band')), parts along dimension 0
- peak_series: float32 [4096], P('beam'), parts along dimension 0
There are 2 independent parts, one for each index of `beam`. A program takes and returns all parts, laid end to end along the dimension named above; an argument that names none is the same for every part. Nothing has to cross between parts.
Inputs may be any that keep to these rules, and one draw needn't show every extreme that they name: `offsets`: in every section some offset equals 255. Among the 8 widths are 1 and 128.
All inputs are finite; a program needn't handle non-finite values.
Results may differ from a plain program's by a relative error of at most 0.0002.
Values sent between devices are 32-bit elements; how exact they have to be, the bound alone decides.
No kernel may reach another device: no remote copies, remote signals or barrier semaphores. Data moves between devices by JAX's collectives and lax.ppermute only.
A program may use at most 64 MiB of HBM per device.

v0:
```python
import math
import jax
import jax.numpy as jnp
from jax import lax
from jax.sharding import PartitionSpec as P

TS = 2048
TIN = 6144
SHIFT = 256
TAPS = 128
TEMPLATES = 8


def from_partner(value, axis, distance):
    mask = 2**distance
    pairs = [(source, source ^ mask) for source in range(lax.axis_size(axis))]
    return lax.ppermute(value, axis, pairs)


def shift_rows(trial_rows, amounts, length):
    current = jnp.pad(trial_rows, ((0, 0), (0, 2 * SHIFT)))
    top_bit = (SHIFT - 1).bit_length()
    for bit_index in reversed(range(top_bit)):
        span = 2**bit_index
        keep_len = length + span - 1
        chosen = (amounts >> bit_index & 1)[:, None] == 1
        current = jnp.where(chosen, current[:, span : span + keep_len], current[:, :keep_len])
    return current


def merge_section(current, offsets_now, section_index, new_length):
    group_trials = 2**section_index
    total_rows = current.shape[0]
    groups = total_rows // (2 * group_trials)
    blocks = current.reshape(groups, 2, group_trials, current.shape[1])
    lower_part = blocks[:, 0, :, :new_length]
    upper_flat = blocks[:, 1].reshape(groups * group_trials, current.shape[1])
    amounts = offsets_now.reshape(groups, 2, group_trials)
    first_half = lower_part + shift_rows(upper_flat, amounts[:, 0].reshape(-1), new_length).reshape(
        groups, group_trials, new_length
    )
    second_half = lower_part + shift_rows(
        upper_flat, amounts[:, 1].reshape(-1), new_length
    ).reshape(groups, group_trials, new_length)
    return jnp.stack([first_half, second_half], axis=1).reshape(total_rows, new_length)


def template_tables(widths):
    source = lax.broadcasted_iota(jnp.int32, (2 * TAPS, TAPS), 0)
    target = lax.broadcasted_iota(jnp.int32, (2 * TAPS, TAPS), 1)
    tap_offset = source - target
    inside = (tap_offset[None] >= 0) & (tap_offset[None] < widths[:, None, None])
    tap_scale = 1.0 / jnp.sqrt(widths.astype(jnp.float32))
    return jnp.where(inside, tap_scale[:, None, None], jnp.zeros((), jnp.float32))


def boxcar_max(dedispersed, widths):
    total_rows = dedispersed.shape[0]
    blocks_time = TS // TAPS
    window = dedispersed.reshape(total_rows, blocks_time + 1, TAPS)
    paired = jnp.concatenate([window[:, :-1], window[:, 1:]], axis=2).reshape(
        total_rows * blocks_time, 2 * TAPS
    )
    tables = template_tables(widths)
    best_value = None
    for template_index in range(TEMPLATES):
        result = jnp.dot(
            paired,
            tables[template_index],
            precision=lax.Precision.HIGHEST,
            preferred_element_type=jnp.float32,
        )
        if template_index == 0:
            best_value = result
        else:
            best_value = jnp.maximum(best_value, result)
    return best_value.reshape(total_rows, TS)


def per_device(filterbank, offsets, widths):
    levels = offsets.shape[0]
    local_count = filterbank.shape[0].bit_length() - 1
    band_count = lax.axis_size("band")
    channels_all = filterbank.shape[0] * band_count

    def length_after(sections_done):
        needed = TS + TAPS + (levels - sections_done) * (SHIFT - 1)
        needed = -(-needed // 128) * 128
        return min(TIN, needed)

    partial_value = jnp.sum(filterbank, axis=0)
    channel_mean = lax.psum(partial_value, "band") / channels_all
    current = filterbank - channel_mean[None, :]
    for local_section_index in range(local_count):
        current = merge_section(
            current,
            offsets[local_section_index],
            local_section_index,
            length_after(local_section_index + 1),
        )
    band_index = lax.axis_index("band")
    for bit_index in range(band_count.bit_length() - 1):
        section_index = local_count + bit_index
        new_length = length_after(section_index + 1)
        partner = from_partner(current, "band", bit_index)
        upper_half = band_index // 2**bit_index % 2 == 1
        lower_part = jnp.where(upper_half, partner, current)
        upper_part = jnp.where(upper_half, current, partner)
        current = lower_part[:, :new_length] + shift_rows(
            upper_part, offsets[section_index], new_length
        )
    dedispersed = current * (1.0 / math.sqrt(channels_all))
    detection = boxcar_max(dedispersed, widths)
    peak_series = lax.pmax(jnp.max(detection, axis=0), "band")
    return (detection, peak_series)


def solution(mesh):
    placed = (P(("beam", "band"), None), P(None, "band"), P())
    return jax.shard_map(
        per_device,
        mesh=mesh,
        in_specs=placed,
        out_specs=(P(("beam", "band"), None), P("beam")),
        check_vma=False,
    )
```

profile of v0, /device:TPU:0, one launch (start us, length us, event | category | flops | bytes accessed | tf_op | source)
XLA Modules:
  0.0 164.7 jit_solution(757025383159185364)
XLA Ops:
  0.6 1.3 reduce_sum.9
  1.9 62.9 %psum.7 = f32[6144]{0:T(1024)S(1)} all-reduce(f32[6144]{0:T(1024)S(1)} %reduce_sum.9), channel_id=1, replica_groups=mesh['beam'=2,'band'=16] {'band'}, use_global_device_ids=true, to_apply=%region_1.0 | all-reduce | flops 6144 | bytes 49152 | tf_op jit(solution)/shard_map/psum | solution.py:92
  64.9 0.5 reshape.1647
  65.4 0.2 slice.1056
  65.6 0.4 slice.1058
  66.0 0.3 copy-done.2
  69.7 0.4 fusion.24
  70.1 0.2 compare_reduce_fusion.15
  73.5 0.2 slice_select_fusion.36
  73.7 0.2 fusion.5
  74.3 0.3 slice.1092
  74.8 0.2 reshape_squeeze.43
  77.4 0.6 copy_add_fusion.1
  77.9 0.5 pad_maximum_fusion.1
  78.5 0.3 reshape_reshape.10
  78.8 0.3 slice.1126
  81.4 0.6 copy_add_fusion.3
  81.9 0.4 pad_maximum_fusion.2
  82.5 0.2 reshape_reshape.11
  83.6 0.3 slice_select_fusion.89
  84.6 0.2 fusion.10
  86.5 0.2 fusion.14
  86.8 1.7 %collective-permute-done = f32[32,3200]{1,0:T(8,128)S(1)} collective-permute-done((f32[32,3200]{1,0:T(8,128)S(1)}, f32[32,3200]{1,0:T(8,128)S(1)}, u32[]{:S(2)}, u32[]{:S(2)}) %collective-permute-start) | collective-permute-done | bytes 409632 | tf_op jit(solution)/shard_map/ppermute | solution.py:17
  88.6 0.2 slice_select_fusion.5
  88.8 0.2 slice_select_fusion.4
  89.0 0.2 slice_select_fusion.3
  89.2 0.2 slice_select_fusion.2
  89.3 0.2 slice_select_fusion.1
  89.5 0.2 slice_select_fusion
  89.7 0.2 fusion
  90.0 10.8 %collective-permute-done.1 = f32[32,2944]{1,0:T(8,128)S(1)} collective-permute-done((f32[32,2944]{1,0:T(8,128)S(1)}, f32[32,2944]{1,0:T(8,128)S(1)}, u32[]{:S(2)}, u32[]{:S(2)}) %collective-permute-start.1) | collective-permute-done | bytes 376864 | tf_op jit(solution)/shard_map/ppermute | solution.py:17
  101.2 0.2 slice_select_fusion.12
  101.4 0.2 slice_select_fusion.11
  101.9 0.2 fusion.1
  102.2 0.6 copy-done.3
  102.9 8.5 %collective-permute-done.2 = f32[32,2688]{1,0:T(8,128)S(1)} collective-permute-done((f32[32,2688]{1,0:T(8,128)S(1)}, f32[32,2688]{1,0:T(8,128)S(1)}, u32[]{:S(2)}, u32[]{:S(2)}) %collective-permute-start.2) | collective-permute-done | bytes 344096 | tf_op jit(solution)/shard_map/ppermute | solution.py:17
  112.5 0.2 fusion.2
  112.8 0.2 and_select_fusion
  113.0 14.9 %collective-permute-done.3 = f32[32,2432]{1,0:T(8,128)S(1)} collective-permute-done((f32[32,2432]{1,0:T(8,128)S(1)}, f32[32,2432]{1,0:T(8,128)S(1)}, u32[]{:S(2)}, u32[]{:S(2)}) %collective-permute-start.3) | collective-permute-done | bytes 311328 | tf_op jit(solution)/shard_map/ppermute | solution.py:17
  129.3 0.6 fusion.15
  129.9 0.6 convolution_maximum_fusion.6
  130.5 0.6 convolution_maximum_fusion.5
  131.0 0.6 convolution_maximum_fusion.4
  131.6 0.6 convolution_maximum_fusion.3
  132.2 0.6 convolution_maximum_fusion.2
  132.8 0.6 convolution_maximum_fusion.1
  133.4 0.6 convolution_maximum_fusion
  134.1 30.6 %pmax.7 = f32[2048]{0:T(1024)} all-reduce(f32[2048]{0:T(1024)S(1)} %reduce_max.9), channel_id=1, replica_groups=mesh['beam'=2,'band'=16] {'band'}, use_global_device_ids=true, to_apply=%region_3.4 | all-reduce | flops 2048 | bytes 16384 | tf_op jit(solution)/shard_map/pmax | solution.py:114
  (188 shorter events, 18.4 us)
Async XLA Ops:
  0.6 64.2 %copy-start = (f32[32,6144]{1,0:T(8,128)S(1)}, f32[32,6144]{1,0:T(8,128)}, u32[]{:S(2)}) copy-start(f32[32,6144]{1,0:T(8,128)} %param.3) | copy-start | bytes 2359300
  65.6 0.7 copy-start.2
  86.7 1.8 %collective-permute-start = (f32[32,3200]{1,0:T(8,128)S(1)}, f32[32,3200]{1,0:T(8,128)S(1)}, u32[]{:S(2)}, u32[]{:S(2)}) collective-permute-start(f32[32,3200]{1,0:T(8,128)S(1)} %bitcast.180), channel_id=1, source_target_pairs={{0,1},{1,0},{2,3},{3,2},{4,5},{5,4},{6,7},{7,6},{8,9},{9,8},{10,11... | collective-permute-start | bytes 1228808 | tf_op jit(solution)/shard_map/ppermute | solution.py:17
  89.9 10.9 %collective-permute-start.1 = (f32[32,2944]{1,0:T(8,128)S(1)}, f32[32,2944]{1,0:T(8,128)S(1)}, u32[]{:S(2)}, u32[]{:S(2)}) collective-permute-start(f32[32,2944]{1,0:T(8,128)S(1)} %fusion), channel_id=1, source_target_pairs={{0,2},{1,3},{2,0},{3,1},{4,6},{5,7},{6,4},{7,5},{8,10},{9,11},{10,... | collective-permute-start | bytes 1130504 | tf_op jit(solution)/shard_map/ppermute | solution.py:17
  102.1 9.3 %collective-permute-start.2 = (f32[32,2688]{1,0:T(8,128)S(1)}, f32[32,2688]{1,0:T(8,128)S(1)}, u32[]{:S(2)}, u32[]{:S(2)}) collective-permute-start(f32[32,2688]{1,0:T(8,128)S(1)} %fusion.1), channel_id=1, source_target_pairs={{0,4},{1,5},{2,6},{3,7},{4,0},{5,1},{6,2},{7,3},{8,12},{9,13},{10,... | collective-permute-start | bytes 1032200 | tf_op jit(solution)/shard_map/ppermute | solution.py:17
  102.2 0.7 copy-start.3
  112.7 15.3 %collective-permute-start.3 = (f32[32,2432]{1,0:T(8,128)S(1)}, f32[32,2432]{1,0:T(8,128)S(1)}, u32[]{:S(2)}, u32[]{:S(2)}) collective-permute-start(f32[32,2432]{1,0:T(8,128)S(1)} %fusion.2), channel_id=1, source_target_pairs={{0,8},{1,9},{2,10},{3,11},{4,12},{5,13},{6,14},{7,15},{8,0},{9,1},... | collective-permute-start | bytes 933896 | tf_op jit(solution)/shard_map/ppermute | solution.py:17
  134.0 30.6 %copy-start.1 = (f32[32,2048]{1,0:T(8,128)}, f32[32,2048]{1,0:T(8,128)S(1)}, u32[]{:S(2)}) copy-start(f32[32,2048]{1,0:T(8,128)S(1)} %reshape.1657) | copy-start | bytes 786436
where the time goes:
time: 165 us
  blocking collectives  93.5 us (57%)
  waiting for transfers between devices  35.9 us (22%)
  other arithmetic  19.1 us (12%)
  local copies, waits for them, and re-layouts  9.32 us (6%)
  matrix products  4.65 us (3%)
  between operations  1.91 us (1%)
    psum x1, blocking collectives, per_device(): channel_mean = lax.psum(partial_value, 'band') / channels_all  62.9 us
    ppermute x4, waiting for transfers between devices, from_partner(): return lax.ppermute(value, axis, pairs)  35.9 us
    pmax x1, blocking collectives, per_device(): peak_series = lax.pmax(jnp.max(detection, axis=0), 'band')  30.6 us
    select_n x96, other arithmetic, shift_rows(): jnp.where(chosen, current[:, span:span + keep_len], current[:, :keep_len])  13 us
    dot_general x8, matrix products, boxcar_max(): jnp.dot(paired, tables[template_index], precision=lax.Precision.HIGHEST,...  4.65 us
    eq x48, local copies, waits for them, and re-layouts, shift_rows(): chosen = (amounts >> bit_index & 1)[:, None] == 1  4.15 us
  transfers between devices with their start and end apart: 4, of which 4 were waited for; matrix products, arithmetic and copies ran while one was open for 0% of the time, Pallas kernels for 0%

commit v1 on v0

--- a/solution.py
+++ b/solution.py
@@ -89,7 +89,7 @@
         return min(TIN, needed)
 
     partial_value = jnp.sum(filterbank, axis=0)
-    channel_mean = lax.psum(partial_value, "band") / channels_all
+    channel_mean = jnp.sum(lax.all_gather(partial_value, "band"), axis=0) / channels_all
     current = filterbank - channel_mean[None, :]
     for local_section_index in range(local_count):
         current = merge_section(

time: 165 us -> 127 us (0.77)
  blocking collectives: 93.5 us -> 54.8 us
    psum x1 -> x0, blocking collectives: 62.9 us -> none  [per_device(): channel_mean = lax.psum(partial_value, 'band') / channels_all]
    all_gather x0 -> x1, blocking collectives: none -> 24.3 us  [per_device(): lax.all_gather(partial_value, 'band')]
where the time goes in v1:
time: 127 us
  blocking collectives  54.8 us (43%)
  waiting for transfers between devices  36.3 us (29%)
  other arithmetic  19.1 us (15%)
  local copies, waits for them, and re-layouts  9.38 us (7%)
  matrix products  4.66 us (4%)
  between operations  1.91 us (2%)
    ppermute x4, waiting for transfers between devices, from_partner(): return lax.ppermute(value, axis, pairs)  36.3 us
    pmax x1, blocking collectives, per_device(): peak_series = lax.pmax(jnp.max(detection, axis=0), 'band')  30.6 us
    all_gather x1, blocking collectives, per_device(): lax.all_gather(partial_value, 'band')  24.3 us
    select_n x96, other arithmetic, shift_rows(): jnp.where(chosen, current[:, span:span + keep_len], current[:, :keep_len])  13 us
    dot_general x8, matrix products, boxcar_max(): jnp.dot(paired, tables[template_index], precision=lax.Precision.HIGHEST,...  4.66 us
    eq x48, local copies, waits for them, and re-layouts, shift_rows(): chosen = (amounts >> bit_index & 1)[:, None] == 1  4.15 us
  transfers between devices with their start and end apart: 4, of which 4 were waited for; matrix products, arithmetic and copies ran while one was open for 0% of the time, Pallas kernels for 0%

profile of v1, /device:TPU:0, one launch (start us, length us, event | category | flops | bytes accessed | tf_op | source)
XLA Modules:
  0.0 126.8 jit_solution(3325731299199960928)
XLA Ops:
  0.6 1.2 reduce_sum.18
  1.9 24.3 %all-gather = f32[98304]{0:T(1024)S(1)} all-gather(f32[6144]{0:T(1024)S(1)} %reduce_sum.18), channel_id=2, replica_groups=mesh['beam'=2,'band'=16] {'band'}, dimensions={0}, use_global_device_ids=true | all-gather | bytes 417792 | tf_op jit(solution)/shard_map/all_gather | solution.py:92
  26.4 0.5 reshape.1649
  26.8 0.2 slice.1056
  27.0 0.4 slice.1058
  27.4 0.3 copy-done.2
  31.1 0.4 fusion.24
  31.6 0.2 compare_reduce_fusion.15
  34.9 0.2 slice_select_fusion.36
  35.2 0.2 fusion.5
  35.8 0.3 slice.1092
  36.2 0.2 reshape_squeeze.43
  38.8 0.6 copy_add_fusion.1
  39.4 0.5 pad_maximum_fusion.1
  39.9 0.3 reshape_reshape.10
  40.2 0.3 slice.1126
  42.8 0.6 copy_add_fusion.3
  43.4 0.4 pad_maximum_fusion.2
  43.9 0.2 reshape_reshape.11
  44.5 0.3 slice_select_fusion.93
  46.0 0.2 fusion.10
  47.9 0.2 fusion.14
  48.1 0.4 collective-permute-start
  48.6 1.3 %collective-permute-done = f32[32,3200]{1,0:T(8,128)S(1)} collective-permute-done((f32[32,3200]{1,0:T(8,128)S(1)}, f32[32,3200]{1,0:T(8,128)S(1)}, u32[]{:S(2)}, u32[]{:S(2)}) %collective-permute-start) | collective-permute-done | bytes 409632 | tf_op jit(solution)/shard_map/ppermute | solution.py:17
  50.1 0.2 slice_select_fusion.5
  50.2 0.2 slice_select_fusion.4
  50.4 0.2 slice_select_fusion.3
  50.6 0.2 slice_select_fusion.2
  50.8 0.2 slice_select_fusion.1
  50.9 0.2 slice_select_fusion
  51.1 0.2 fusion
  51.4 11.0 %collective-permute-done.1 = f32[32,2944]{1,0:T(8,128)S(1)} collective-permute-done((f32[32,2944]{1,0:T(8,128)S(1)}, f32[32,2944]{1,0:T(8,128)S(1)}, u32[]{:S(2)}, u32[]{:S(2)}) %collective-permute-start.1) | collective-permute-done | bytes 376864 | tf_op jit(solution)/shard_map/ppermute | solution.py:17
  62.9 0.2 slice_select_fusion.12
  63.5 0.2 fusion.1
  63.9 0.6 copy-done.3
  64.5 8.8 %collective-permute-done.2 = f32[32,2688]{1,0:T(8,128)S(1)} collective-permute-done((f32[32,2688]{1,0:T(8,128)S(1)}, f32[32,2688]{1,0:T(8,128)S(1)}, u32[]{:S(2)}, u32[]{:S(2)}) %collective-permute-start.2) | collective-permute-done | bytes 344096 | tf_op jit(solution)/shard_map/ppermute | solution.py:17
  74.4 0.2 fusion.2
  74.6 0.2 and_select_fusion
  74.9 15.2 %collective-permute-done.3 = f32[32,2432]{1,0:T(8,128)S(1)} collective-permute-done((f32[32,2432]{1,0:T(8,128)S(1)}, f32[32,2432]{1,0:T(8,128)S(1)}, u32[]{:S(2)}, u32[]{:S(2)}) %collective-permute-start.3) | collective-permute-done | bytes 311328 | tf_op jit(solution)/shard_map/ppermute | solution.py:17
  91.4 0.6 fusion.15
  92.0 0.6 convolution_maximum_fusion.6
  92.6 0.6 convolution_maximum_fusion.5
  93.2 0.6 convolution_maximum_fusion.4
  93.8 0.6 convolution_maximum_fusion.3
  94.3 0.6 convolution_maximum_fusion.2
  94.9 0.6 convolution_maximum_fusion.1
  95.5 0.6 convolution_maximum_fusion
  96.2 30.6 %pmax.7 = f32[2048]{0:T(1024)} all-reduce(f32[2048]{0:T(1024)S(1)} %reduce_max.9), channel_id=1, replica_groups=mesh['beam'=2,'band'=16] {'band'}, use_global_device_ids=true, to_apply=%region_3.4 | all-reduce | flops 2048 | bytes 16384 | tf_op jit(solution)/shard_map/pmax | solution.py:114
  (190 shorter events, 18.6 us)
Async XLA Ops:
  1.8 24.4 %copy-start = (f32[32,6144]{1,0:T(8,128)S(1)}, f32[32,6144]{1,0:T(8,128)}, u32[]{:S(2)}) copy-start(f32[32,6144]{1,0:T(8,128)} %param.3) | copy-start | bytes 2359300
  27.0 0.7 copy-start.2
  48.1 1.8 %collective-permute-start = (f32[32,3200]{1,0:T(8,128)S(1)}, f32[32,3200]{1,0:T(8,128)S(1)}, u32[]{:S(2)}, u32[]{:S(2)}) collective-permute-start(f32[32,3200]{1,0:T(8,128)S(1)} %bitcast.180), channel_id=1, source_target_pairs={{0,1},{1,0},{2,3},{3,2},{4,5},{5,4},{6,7},{7,6},{8,9},{9,8},{10,11... | collective-permute-start | bytes 1228808 | tf_op jit(solution)/shard_map/ppermute | solution.py:17
  51.3 11.1 %collective-permute-start.1 = (f32[32,2944]{1,0:T(8,128)S(1)}, f32[32,2944]{1,0:T(8,128)S(1)}, u32[]{:S(2)}, u32[]{:S(2)}) collective-permute-start(f32[32,2944]{1,0:T(8,128)S(1)} %fusion), channel_id=1, source_target_pairs={{0,2},{1,3},{2,0},{3,1},{4,6},{5,7},{6,4},{7,5},{8,10},{9,11},{10,... | collective-permute-start | bytes 1130504 | tf_op jit(solution)/shard_map/ppermute | solution.py:17
  63.7 9.6 %collective-permute-start.2 = (f32[32,2688]{1,0:T(8,128)S(1)}, f32[32,2688]{1,0:T(8,128)S(1)}, u32[]{:S(2)}, u32[]{:S(2)}) collective-permute-start(f32[32,2688]{1,0:T(8,128)S(1)} %fusion.1), channel_id=1, source_target_pairs={{0,4},{1,5},{2,6},{3,7},{4,0},{5,1},{6,2},{7,3},{8,12},{9,13},{10,... | collective-permute-start | bytes 1032200 | tf_op jit(solution)/shard_map/ppermute | solution.py:17
  63.8 0.7 copy-start.3
  74.5 15.5 %collective-permute-start.3 = (f32[32,2432]{1,0:T(8,128)S(1)}, f32[32,2432]{1,0:T(8,128)S(1)}, u32[]{:S(2)}, u32[]{:S(2)}) collective-permute-start(f32[32,2432]{1,0:T(8,128)S(1)} %fusion.2), channel_id=1, source_target_pairs={{0,8},{1,9},{2,10},{3,11},{4,12},{5,13},{6,14},{7,15},{8,0},{9,1},... | collective-permute-start | bytes 933896 | tf_op jit(solution)/shard_map/ppermute | solution.py:17
  96.2 30.6 %copy-start.1 = (f32[32,2048]{1,0:T(8,128)}, f32[32,2048]{1,0:T(8,128)S(1)}, u32[]{:S(2)}) copy-start(f32[32,2048]{1,0:T(8,128)S(1)} %reshape.1659) | copy-start | bytes 786436
